TPU v7x, 32 devices: a whole 2x2x4 slice. The times are simulated.
32 devices in a mesh: row: 8 (over z, core), col: 4 (over y, x).
Axes of the slice: x: 2, y: 2, z: 4, core: 2. Of those that a mesh axis runs over, the one named last changes fastest.
Arguments:
- activations: bfloat16 [1024, 8192], P('col', 'row'), may hold values from -6 to 6
- out_grad: bfloat16 [1024, 8192], P('col', 'row'), may hold values from -6 to 6
- gate_pre: bfloat16 [1024, 16384], P('row', 'col'), may hold values from -8 to 8
- up_proj: bfloat16 [1024, 16384], P('row', 'col'), may hold values from -6 to 6
- gate_weight: bfloat16 [8192, 16384], P('row', 'col'), may hold values from -0.0625 to 0.0625
- up_weight: bfloat16 [8192, 16384], P('row', 'col'), may hold values from -0.0625 to 0.0625
- down_weight: bfloat16 [16384, 8192], P('col', 'row'), may hold values from -0.046875 to 0.046875
Outputs:
- input_grad: bfloat16 [1024, 8192], P('col', 'row')
- gate_grad: bfloat16 [8192, 16384], P('row', 'col')
- up_grad: bfloat16 [8192, 16384], P('row', 'col')
- down_grad: bfloat16 [16384, 8192], P('col', 'row')
All inputs are finite; a program needn't handle non-finite values.
Results may differ from a plain program's by a relative error of at most 0.0051.
Values may be sent and summed in bfloat16 or wider, within the bound.
No kernel may reach another device: no remote copies, remote signals or barrier semaphores. Data moves between devices by JAX's collectives and lax.ppermute only.
A program may use at most 192 MiB of HBM per device.

v0:
```python
import jax
import jax.numpy as jnp
from jax import lax
from jax.sharding import PartitionSpec as P


def local_grads(gate_rows, up_rows, grad_rows):
    gate_float = gate_rows.astype(jnp.float32)
    up_float = up_rows.astype(jnp.float32)
    sigmoid_gate = jax.nn.sigmoid(gate_float)
    silu_gate = gate_float * sigmoid_gate
    hidden_act = (silu_gate * up_float).astype(jnp.bfloat16)
    gate_delta = (
        grad_rows * up_float * sigmoid_gate * (1.0 + gate_float * (1.0 - sigmoid_gate))
    ).astype(jnp.bfloat16)
    up_delta = (grad_rows * silu_gate).astype(jnp.bfloat16)
    return (hidden_act, gate_delta, up_delta)


def body(activations, out_grad, gate_pre, up_proj, gate_weight, up_weight, down_weight):
    act_full, grad_full = (
        lax.all_gather(activations, "col", axis=0, tiled=True),
        lax.all_gather(out_grad, "col", axis=0, tiled=True),
    )
    tokens_all = act_full.shape[0]
    contract_last = (((1,), (1,)), ((), ()))
    contract_first = (((0,), (0,)), ((), ()))
    grad_rows = grad_full
    hid_rows = lax.psum_scatter(
        lax.dot_general(grad_rows, down_weight, contract_last, preferred_element_type=jnp.float32),
        "row",
        scatter_dimension=0,
        tiled=True,
    )
    products = local_grads(gate_pre, up_proj, hid_rows)
    hidden_act = lax.all_gather(products[0], "row", axis=0, tiled=True)
    gate_delta = lax.all_gather(products[1], "row", axis=0, tiled=True)
    up_delta = lax.all_gather(products[2], "row", axis=0, tiled=True)
    grad_rows = grad_full
    acc_down = lax.dot_general(
        hidden_act, grad_rows, contract_first, preferred_element_type=jnp.float32
    )
    acc_gate = lax.dot_general(
        act_full, gate_delta, contract_first, preferred_element_type=jnp.float32
    )
    acc_up = lax.dot_general(act_full, up_delta, contract_first, preferred_element_type=jnp.float32)
    input_rows = lax.dot_general(
        gate_delta, gate_weight, contract_last, preferred_element_type=jnp.float32
    )
    input_rows = input_rows + lax.dot_general(
        up_delta, up_weight, contract_last, preferred_element_type=jnp.float32
    )
    acc_input = input_rows
    totals = (acc_down, acc_gate, acc_up, acc_input)
    acc_down, acc_gate, acc_up, acc_input = totals
    input_rows = lax.psum_scatter(acc_input, "col", scatter_dimension=0, tiled=True).astype(
        jnp.bfloat16
    )
    factor = float(tokens_all) ** (-0.5)
    return (
        input_rows,
        (acc_gate * factor).astype(jnp.bfloat16),
        (acc_up * factor).astype(jnp.bfloat16),
        (acc_down * factor).astype(jnp.bfloat16),
    )


def solution(mesh):
    in_specs = (
        P("col", "row"),
        P("col", "row"),
        P("row", "col"),
        P("row", "col"),
        P("row", "col"),
        P("row", "col"),
        P("col", "row"),
    )
    out_specs = (P("col", "row"), P("row", "col"), P("row", "col"), P("col", "row"))
    return jax.shard_map(body, mesh=mesh, in_specs=in_specs, out_specs=out_specs, check_vma=False)
```

profile of v0, /device:TPU:0, one launch (start us, length us, event | category | flops | bytes accessed | tf_op | source)
XLA Modules:
  0.0 582.2 jit_solution(11149804209979248327)
XLA Ops:
  7.2 0.7 all-gather.6.cloned.1.call-update
  7.9 39.9 %all-gather.6.cloned.1.call-done = bf16[1024,1024]{1,0:T(8,128)(2,1)} async-done(((bf16[256,1024]{1,0:T(8,128)(2,1)}), bf16[1024,1024]{1,0:T(8,128)(2,1)}) %all-gather.6.cloned.1.call-update) | async-done | bytes 2097168 | tf_op jit(solution)/shard_map/all_gather | solution.py:23
  47.9 16.0 %fusion.10 = f32[1024,4096]{1,0:T(8,128)} fusion(bf16[1024,1024]{1,0:T(8,128)(2,1)} %all-gather.6.cloned.1.call-done, bf16[4096,1024]{1,0:T(8,128)(2,1)} %param.13), kind=kOutput, calls=%fused_computation.20 | convolution fusion | flops 8589934592 | bytes 27262976 | tf_op jit(solution)/shard_map/dot_general | solution.py:30
  64.0 0.0 all-gather.8.cloned.1.call-start
  64.0 168.3 %reduce-scatter.3.cloned.1.call-done = f32[128,4096]{1,0:T(8,128)} async-done(((f32[1024,4096]{1,0:T(8,128)}), f32[128,4096]{1,0:T(8,128)}) %reduce-scatter.3.cloned.1.call-update) | async-done | bytes 2097168 | tf_op jit(solution)/shard_map/reduce_scatter | solution.py:29
  232.4 4.4 multiply_convert_fusion.3
  236.8 0.0 all-gather.10.cloned.1.call-start
  236.8 0.5 all-gather.10.cloned.1.call-update
  237.4 0.5 all-gather.12.cloned.1.call-update
  238.0 0.5 all-gather.14.cloned.1.call-update
  238.5 0.2 reduce-scatter.5.cloned.1.call-start
  238.7 78.6 %all-gather.8.cloned.1.call-done = bf16[1024,4096]{1,0:T(8,128)(2,1)} async-done(((bf16[128,4096]{1,0:T(8,128)(2,1)}), bf16[1024,4096]{1,0:T(8,128)(2,1)}) %all-gather.8.cloned.1.call-update) | async-done | bytes 8388624 | tf_op jit(solution)/shard_map/all_gather | solution.py:37
  317.3 15.0 %fusion.11 = f32[1024,1024]{1,0:T(8,128)} fusion(bf16[1024,4096]{1,0:T(8,128)(2,1)} %all-gather.8.cloned.1.call-done, bf16[1024,4096]{1,0:T(8,128)(2,1)} %param.11), kind=kOutput, calls=%fused_computation.21 | convolution fusion | flops 8589934592 | bytes 20971520 | tf_op jit(solution)/shard_map/dot_general | solution.py:47
  332.3 67.6 %all-gather.10.cloned.1.call-done = bf16[1024,4096]{1,0:T(8,128)(2,1)} async-done(((bf16[128,4096]{1,0:T(8,128)(2,1)}), bf16[1024,4096]{1,0:T(8,128)(2,1)}) %all-gather.10.cloned.1.call-update) | async-done | bytes 8388624 | tf_op jit(solution)/shard_map/all_gather | solution.py:38
  400.0 15.7 %convolution_add_fusion = f32[1024,1024]{1,0:T(8,128)} fusion(f32[1024,1024]{1,0:T(8,128)} %fusion.11, bf16[1024,4096]{1,0:T(8,128)(2,1)} %all-gather.10.cloned.1.call-done, bf16[1024,4096]{1,0:T(8,128)(2,1)} %param.12), kind=kOutput, calls=%fused_computation.19 | convolution fusion | flops 8590983168 | bytes 25165824 | tf_op jit(solution)/shard_map/dot_general | solution.py:50
  415.7 19.8 %all-gather.12.cloned.1.call-done = bf16[1024,1024]{1,0:T(8,128)(2,1)} async-done(((bf16[256,1024]{1,0:T(8,128)(2,1)}), bf16[1024,1024]{1,0:T(8,128)(2,1)}) %all-gather.12.cloned.1.call-update) | async-done | bytes 2097168 | tf_op jit(solution)/shard_map/all_gather | solution.py:22
  435.5 14.9 %fusion = bf16[1024,4096]{0,1:T(8,128)(2,1)} fusion(bf16[1024,4096]{1,0:T(8,128)(2,1)} %all-gather.8.cloned.1.call-done, bf16[1024,1024]{1,0:T(8,128)(2,1)} %all-gather.12.cloned.1.call-done), kind=kOutput, calls=%fused_computation.3 | convolution fusion | flops 8598323200 | bytes 18874368 | tf_op jit(solution)/shard_map/dot_general | solution.py:43
  450.4 12.1 %copy.11 = bf16[1024,4096]{1,0:T(8,128)(2,1)} copy(bf16[1024,4096]{0,1:T(8,128)(2,1)} %fusion) | data formatting | bytes 16777216
  462.5 14.7 %fusion.1 = bf16[1024,4096]{0,1:T(8,128)(2,1)} fusion(bf16[1024,4096]{1,0:T(8,128)(2,1)} %all-gather.10.cloned.1.call-done, bf16[1024,1024]{1,0:T(8,128)(2,1)S(1)} %copy-done.3), kind=kOutput, calls=%fused_computation.4 | convolution fusion | flops 8598323200 | bytes 18874368 | tf_op jit(solution)/shard_map/dot_general | solution.py:46
  477.2 12.1 %copy.12 = bf16[1024,4096]{1,0:T(8,128)(2,1)} copy(bf16[1024,4096]{0,1:T(8,128)(2,1)} %fusion.1) | data formatting | bytes 16777216
  489.3 29.8 %all-gather.14.cloned.1.call-done = bf16[1024,4096]{1,0:T(8,128)(2,1)} async-done(((bf16[128,4096]{1,0:T(8,128)(2,1)}), bf16[1024,4096]{1,0:T(8,128)(2,1)}) %all-gather.14.cloned.1.call-update) | async-done | bytes 8388624 | tf_op jit(solution)/shard_map/all_gather | solution.py:36
  519.1 14.6 %multiply_convert_fusion = bf16[4096,1024]{1,0:T(8,128)(2,1)} fusion(bf16[1024,4096]{1,0:T(8,128)(2,1)} %all-gather.14.cloned.1.call-done, bf16[1024,1024]{1,0:T(8,128)(2,1)S(1)} %copy-done.2), kind=kOutput, calls=%fused_computation | convolution fusion | flops 8598323200 | bytes 18874368 | tf_op jit(solution)/shard_map/dot_general | solution.py:40
  533.6 39.7 %reduce-scatter.5.cloned.1.call-done = f32[256,1024]{1,0:T(8,128)} async-done(((f32[1024,1024]{1,0:T(8,128)}), f32[256,1024]{1,0:T(8,128)}) %reduce-scatter.5.cloned.1.call-update) | async-done | bytes 1048592 | tf_op jit(solution)/shard_map/reduce_scatter | solution.py:56
  573.3 2.1 convert_element_type.37
  (15 shorter events, 0.2 us)
Async XLA Ops:
  7.2 40.7 %all-gather.6.cloned.1.call-start = ((), (), s32[]{:S(2)}) async-start(), calls=%async_computation.2 | async-start | bytes 2621440 | tf_op jit(solution)/shard_map/all_gather | solution.py:23
  7.9 224.5 %reduce-scatter.3.cloned.1.call-start = ((), (), s32[]{:S(2)}) async-start(), calls=%async_computation.3 | async-start | bytes 18874368 | tf_op jit(solution)/shard_map/reduce_scatter | solution.py:29
  63.9 168.4 %copy-start = (bf16[128,4096]{1,0:T(8,128)(2,1)S(1)}, bf16[128,4096]{1,0:T(8,128)(2,1)}, u32[]{:S(2)}) copy-start(bf16[128,4096]{1,0:T(8,128)(2,1)} %param.9) | copy-start | bytes 3145732
  63.9 168.4 %copy-start.1 = (bf16[128,4096]{1,0:T(8,128)(2,1)S(1)}, bf16[128,4096]{1,0:T(8,128)(2,1)}, u32[]{:S(2)}) copy-start(bf16[128,4096]{1,0:T(8,128)(2,1)} %param.10) | copy-start | bytes 3145732
  64.0 253.3 %all-gather.8.cloned.1.call-start = ((), (), s32[]{:S(2)}) async-start(), calls=%async_computation.4 | async-start | bytes 9437184 | tf_op jit(solution)/shard_map/all_gather | solution.py:37
  236.8 163.2 %all-gather.10.cloned.1.call-start = ((), (), s32[]{:S(2)}) async-start(), calls=%async_computation.5 | async-start | bytes 9437184 | tf_op jit(solution)/shard_map/all_gather | solution.py:38
  237.3 198.2 %all-gather.12.cloned.1.call-start = ((), (), s32[]{:S(2)}) async-start(), calls=%async_computation.7 | async-start | bytes 2621440 | tf_op jit(solution)/shard_map/all_gather | solution.py:22
  237.9 281.1 %all-gather.14.cloned.1.call-start = ((), (), s32[]{:S(2)}) async-start(), calls=%async_computation.8 | async-start | bytes 9437184 | tf_op jit(solution)/shard_map/all_gather | solution.py:36
  238.5 334.8 %reduce-scatter.5.cloned.1.call-start = ((), (), s32[]{:S(2)}) async-start(), calls=%async_computation.6 | async-start | bytes 5242880 | tf_op jit(solution)/shard_map/reduce_scatter | solution.py:56
  450.4 12.1 %copy-start.3 = (bf16[1024,1024]{1,0:T(8,128)(2,1)S(1)}, bf16[1024,1024]{1,0:T(8,128)(2,1)}, u32[]{:S(2)}) copy-start(bf16[1024,1024]{1,0:T(8,128)(2,1)} %all-gather.12.cloned.1.call-done) | copy-start | bytes 6291460
  477.2 41.9 %copy-start.2 = (bf16[1024,1024]{1,0:T(8,128)(2,1)S(1)}, bf16[1024,1024]{1,0:T(8,128)(2,1)}, u32[]{:S(2)}) copy-start(bf16[1024,1024]{1,0:T(8,128)(2,1)} %all-gather.6.cloned.1.call-done) | copy-start | bytes 6291460
Sparse Core Ops, SparseCore 0:
  9.8 38.0 all-gather.5
  64.1 168.2 reduce-scatter.2
  236.9 80.3 all-gather.7
  319.3 80.5 all-gather.9
  401.6 33.8 all-gather.11
  437.0 82.0 all-gather.13
  522.0 51.2 reduce-scatter.4
where the time goes:
time: 583 us; the launch traced here: 582 us
  waiting for transfers between devices  446 us (77%)
  matrix products  90.9 us (16%)
  local copies, waits for them, and re-layouts  24.2 us (4%)
  between operations  14.1 us (2%)
  other arithmetic  6.46 us (1%)
    reduce_scatter x1, waiting for transfers between devices, body(): lax.psum_scatter(lax.dot_general(grad_rows, down_weight, contract_last, p...  168 us
    all_gather x1, waiting for transfers between devices, body(): gate_delta = lax.all_gather(products[1], 'row', axis=0, tiled=True)  78.6 us
    all_gather x1, waiting for transfers between devices, body(): up_delta = lax.all_gather(products[2], 'row', axis=0, tiled=True)  67.6 us
    all_gather x1, waiting for transfers between devices, body(): lax.all_gather(out_grad, 'col', axis=0, tiled=True)  39.9 us
    reduce_scatter x1, waiting for transfers between devices, body(): lax.psum_scatter(acc_input, 'col', scatter_dimension=0, tiled=True)  39.7 us
    all_gather x1, waiting for transfers between devices, body(): hidden_act = lax.all_gather(products[0], 'row', axis=0, tiled=True)  29.8 us
    unnamed x10, local copies, waits for them, and re-layouts  24.2 us
    all_gather x1, waiting for transfers between devices, body(): lax.all_gather(activations, 'col', axis=0, tiled=True)  19.8 us
  transfers between devices with their start and end apart: 7, of which 7 were waited for; matrix products, arithmetic and copies ran while one was open for 17% of the time, Pallas kernels for 0%

commit v1 on v0

--- a/solution.py
+++ b/solution.py
@@ -2,6 +2,12 @@
 import jax.numpy as jnp
 from jax import lax
 from jax.sharding import PartitionSpec as P
+
+
+def _place_leaves(local_values, row_dim):
+    q_next = list(local_values.shape[1:])
+    q_next[row_dim] *= local_values.shape[0]
+    return jnp.moveaxis(local_values, 0, row_dim).reshape(q_next)
 
 
 def local_grads(gate_rows, up_rows, grad_rows):
@@ -35,7 +41,29 @@
     products = local_grads(gate_pre, up_proj, hid_rows)
     hidden_act = lax.all_gather(products[0], "row", axis=0, tiled=True)
     gate_delta = lax.all_gather(products[1], "row", axis=0, tiled=True)
-    up_delta = lax.all_gather(products[2], "row", axis=0, tiled=True)
+
+    def supply_columns_in(target, axis_tag, along_dim):
+        n_parts = lax.axis_size(axis_tag)
+        passed = range(n_parts)
+        block_now = map(lambda hop_no: (hop_no, (hop_no + 1) % n_parts), passed)
+        chunks = list(block_now)
+        by_rank = [(no, i0) for i0, no in chunks]
+        arr_out, parts_out = ([], [])
+        for i in range(n_parts - 1):
+            if i % 2 == 0:
+                right_arr = lax.ppermute(arr_out[-1] if arr_out else target, axis_tag, chunks)
+                arr_out.append(right_arr)
+            else:
+                formed = lax.ppermute(parts_out[-1] if parts_out else target, axis_tag, by_rank)
+                parts_out.append(formed)
+        view_out = jnp.stack([*arr_out[::-1], target, *parts_out], axis=0)
+        carry_out = lax.axis_index(axis_tag)
+        state_now = len(arr_out)
+        current_value = carry_out - state_now
+        view_out = view_out[(jnp.arange(n_parts) - current_value) % n_parts]
+        return _place_leaves(view_out, along_dim)
+
+    up_delta = supply_columns_in(products[2], "row", 0)
     grad_rows = grad_full
     acc_down = lax.dot_general(
         hidden_act, grad_rows, contract_first, preferred_element_type=jnp.float32

time: 583 us -> 550 us (0.943)
  waiting for transfers between devices: 446 us -> 386 us
  local copies, waits for them, and re-layouts: 24.2 us -> 45.7 us
  starting transfers between devices: 0.45 us -> 11.1 us
    ppermute x0 -> x7, waiting for transfers between devices: none -> 129 us  [the longest x4 120 us: supply_columns_in(): lax.ppermute(arr_out[-1] if arr_out else target, axis_tag, chunks)]
    all_gather x1, waiting for transfers between devices: 78.6 us -> 0.01 us  [body(): gate_delta = lax.all_gather(products[1], 'row', axis=0, tiled=True)]
    all_gather x1 -> x0, waiting for transfers between devices: 67.6 us -> none  [body(): up_delta = lax.all_gather(products[2], 'row', axis=0, tiled=True)]
    all_gather x1, waiting for transfers between devices: 29.8 us -> 7.87 us  [body(): hidden_act = lax.all_gather(products[0], 'row', axis=0, tiled=True)]
    all_gather x1, waiting for transfers between devices: 19.8 us -> 0.02 us  [body(): lax.all_gather(activations, 'col', axis=0, tiled=True)]
    unnamed x10 -> x19, local copies, waits for them, and re-layouts: 24.2 us -> 36.4 us
    ppermute x0 -> x7, starting transfers between devices: none -> 10.9 us  [the longest x3 10.8 us: supply_columns_in(): lax.ppermute(parts_out[-1] if parts_out else target, axis_tag, by_rank)]
    gather x0 -> x1, local copies, waits for them, and re-layouts: none -> 8.23 us  [supply_columns_in(): view_out = view_out[(jnp.arange(n_parts) - current_value) % n_parts]]
  transfers between devices with their start and end apart: 7 -> 13, of which waited for: 7 -> 9; matrix products, arithmetic and copies ran while one was open for 17% -> 21% of each run, Pallas kernels for 0% -> 0%
where the time goes in v1:
time: 550 us
  waiting for transfers between devices  386 us (70%)
  matrix products  86.3 us (16%)
  local copies, waits for them, and re-layouts  45.7 us (8%)
  between operations  14.2 us (3%)
  starting transfers between devices  11.1 us (2%)
  other arithmetic  6.26 us (1%)
    reduce_scatter x1, waiting for transfers between devices, body(): lax.psum_scatter(lax.dot_general(grad_rows, down_weight, contract_last, p...  168 us
    ppermute x4, waiting for transfers between devices, supply_columns_in(): lax.ppermute(arr_out[-1] if arr_out else target, axis_tag, chunks)  120 us
    all_gather x1, waiting for transfers between devices, body(): lax.all_gather(out_grad, 'col', axis=0, tiled=True)  39.9 us
    reduce_scatter x1, waiting for transfers between devices, body(): lax.psum_scatter(acc_input, 'col', scatter_dimension=0, tiled=True)  39.5 us
    unnamed x19, local copies, waits for them, and re-layouts  36.4 us
    dot_general x1, matrix products, body(): lax.dot_general(grad_rows, down_weight, contract_last, preferred_element_...  16 us
    dot_general x1, matrix products, body(): lax.dot_general(act_full, up_delta, contract_first, preferred_element_typ...  15.2 us
    dot_general x1, matrix products, body(): lax.dot_general(act_full, gate_delta, contract_first, preferred_element_t...  14.7 us
  transfers between devices with their start and end apart: 13, of which 9 were waited for; matrix products, arithmetic and copies ran while one was open for 21% of the time, Pallas kernels for 0%

profile of v1, /device:TPU:0, one launch (start us, length us, event | category | flops | bytes accessed | tf_op | source)
XLA Modules:
  0.0 549.5 jit_solution(125617500321907077)
XLA Ops:
  7.9 39.9 %all-gather.5.cloned.1.call-done = bf16[1024,1024]{1,0:T(8,128)(2,1)} async-done(((bf16[256,1024]{1,0:T(8,128)(2,1)}), bf16[1024,1024]{1,0:T(8,128)(2,1)}) %all-gather.5.cloned.1.call-update) | async-done | bytes 2097168 | tf_op jit(solution)/shard_map/all_gather | solution.py:29
  47.9 16.0 %fusion.12 = f32[1024,4096]{1,0:T(8,128)} fusion(bf16[1024,1024]{1,0:T(8,128)(2,1)} %all-gather.5.cloned.1.call-done, bf16[4096,1024]{1,0:T(8,128)(2,1)} %param.13), kind=kOutput, calls=%fused_computation.36 | convolution fusion | flops 8589934592 | bytes 27262976 | tf_op jit(solution)/shard_map/dot_general | solution.py:36
  64.0 168.3 %reduce-scatter.3.cloned.1.call-done = f32[128,4096]{1,0:T(8,128)} async-done(((f32[1024,4096]{1,0:T(8,128)}), f32[128,4096]{1,0:T(8,128)}) %reduce-scatter.3.cloned.1.call-update) | async-done | bytes 2097168 | tf_op jit(solution)/shard_map/reduce_scatter | solution.py:35
  232.4 4.1 multiply_convert_fusion.3
  237.2 26.8 %collective-permute-done = bf16[128,4096]{1,0:T(8,128)(2,1)S(1)} collective-permute-done((bf16[128,4096]{1,0:T(8,128)(2,1)S(1)}, bf16[128,4096]{1,0:T(8,128)(2,1)S(1)}, u32[]{:S(2)}, u32[]{:S(2)}) %collective-permute-start) | collective-permute-done | bytes 1048608 | tf_op jit(solution)/shard_map/ppermute | solution.py:54
  264.1 3.6 collective-permute-start.4
  267.6 45.6 %collective-permute-done.1 = bf16[128,4096]{1,0:T(8,128)(2,1)S(1)} collective-permute-done((bf16[128,4096]{1,0:T(8,128)(2,1)S(1)}, bf16[128,4096]{1,0:T(8,128)(2,1)S(1)}, u32[]{:S(2)}, u32[]{:S(2)}) %collective-permute-start.1) | collective-permute-done | bytes 1048608 | tf_op jit(solution)/shard_map/ppermute | solution.py:54
  313.3 3.5 collective-permute-start.5
  316.8 36.1 %collective-permute-done.2 = bf16[128,4096]{1,0:T(8,128)(2,1)} collective-permute-done((bf16[128,4096]{1,0:T(8,128)(2,1)S(1)}, bf16[128,4096]{1,0:T(8,128)(2,1)}, u32[]{:S(2)}, u32[]{:S(2)}) %collective-permute-start.2) | collective-permute-done | bytes 1048608 | tf_op jit(solution)/shard_map/ppermute | solution.py:54
  353.0 9.0 %collective-permute-done.5 = bf16[128,4096]{1,0:T(8,128)(2,1)} collective-permute-done((bf16[128,4096]{1,0:T(8,128)(2,1)}, bf16[128,4096]{1,0:T(8,128)(2,1)}, u32[]{:S(2)}, u32[]{:S(2)}) %collective-permute-start.5) | collective-permute-done | bytes 1048608 | tf_op jit(solution)/shard_map/ppermute | solution.py:57
  362.0 3.7 collective-permute-start.6
  365.7 11.4 %collective-permute-done.3 = bf16[128,4096]{1,0:T(8,128)(2,1)} collective-permute-done((bf16[128,4096]{1,0:T(8,128)(2,1)}, bf16[128,4096]{1,0:T(8,128)(2,1)}, u32[]{:S(2)}, u32[]{:S(2)}) %collective-permute-start.3) | collective-permute-done | bytes 1048608 | tf_op jit(solution)/shard_map/ppermute | solution.py:54
  377.1 2.3 bitcast_dynamic-update-slice_fusion.7
  379.4 2.3 bitcast_dynamic-update-slice_fusion.6
  390.4 8.2 %gather_fusion = bf16[8,128,4096]{2,1,0:T(8,128)(2,1)} fusion(bf16[8,128,4096]{2,1,0:T(8,128)(2,1)} %bitcast_dynamic-update-slice_fusion, s32[1024]{0:T(1024)S(1)} %pad_clamp_fusion), kind=kCustom, calls=%fused_computation | custom fusion | bytes 16777248 | tf_op jit(solution)/shard_map/gather | solution.py:63
  398.7 12.8 %fusion.13 = f32[1024,1024]{1,0:T(8,128)S(1)} fusion(bf16[1024,4096]{1,0:T(8,128)(2,1)} %all-gather.7.cloned.1.call-done, bf16[1024,4096]{1,0:T(8,128)(2,1)} %param.11), kind=kOutput, calls=%fused_computation.37 | convolution fusion | flops 8589934592 | bytes 20971520 | tf_op jit(solution)/shard_map/dot_general | solution.py:75
  411.5 13.0 %convolution_add_fusion = f32[1024,1024]{1,0:T(8,128)} fusion(f32[1024,1024]{1,0:T(8,128)S(1)} %fusion.13, bf16[1024,4096]{1,0:T(8,128)(2,1)S(1)} %bitcast.36, bf16[1024,4096]{1,0:T(8,128)(2,1)} %param.12), kind=kOutput, calls=%fused_computation.20 | convolution fusion | flops 8590983168 | bytes 25165824 | tf_op jit(solution)/shard_map/dot_general | solution.py:78
  424.6 15.2 %fusion.1 = bf16[1024,4096]{0,1:T(8,128)(2,1)} fusion(bf16[1024,4096]{1,0:T(8,128)(2,1)} %bitcast.35, bf16[1024,1024]{1,0:T(8,128)(2,1)} %all-gather.9.cloned.1.call-done), kind=kOutput, calls=%fused_computation.5 | convolution fusion | flops 8598323200 | bytes 18874368 | tf_op jit(solution)/shard_map/dot_general | solution.py:74
  439.8 12.1 %copy.12 = bf16[1024,4096]{1,0:T(8,128)(2,1)} copy(bf16[1024,4096]{0,1:T(8,128)(2,1)} %fusion.1) | data formatting | bytes 16777216
  451.9 14.7 %fusion = bf16[1024,4096]{0,1:T(8,128)(2,1)} fusion(bf16[1024,4096]{1,0:T(8,128)(2,1)} %all-gather.7.cloned.1.call-done, bf16[1024,1024]{1,0:T(8,128)(2,1)S(1)} %copy-done.4), kind=kOutput, calls=%fused_computation.4 | convolution fusion | flops 8598323200 | bytes 18874368 | tf_op jit(solution)/shard_map/dot_general | solution.py:71
  466.6 12.1 %copy.11 = bf16[1024,4096]{1,0:T(8,128)(2,1)} copy(bf16[1024,4096]{0,1:T(8,128)(2,1)} %fusion) | data formatting | bytes 16777216
  478.6 7.9 %all-gather.11.cloned.1.call-done = bf16[1024,4096]{1,0:T(8,128)(2,1)} async-done(((bf16[128,4096]{1,0:T(8,128)(2,1)}), bf16[1024,4096]{1,0:T(8,128)(2,1)}) %all-gather.11.cloned.1.call-update) | async-done | bytes 8388624 | tf_op jit(solution)/shard_map/all_gather | solution.py:42
  486.5 14.6 %multiply_convert_fusion = bf16[4096,1024]{1,0:T(8,128)(2,1)} fusion(bf16[1024,4096]{1,0:T(8,128)(2,1)} %all-gather.11.cloned.1.call-done, bf16[1024,1024]{1,0:T(8,128)(2,1)S(1)} %copy-done.3), kind=kOutput, calls=%fused_computation.1 | convolution fusion | flops 8598323200 | bytes 18874368 | tf_op jit(solution)/shard_map/dot_general | solution.py:68
  501.1 39.5 %reduce-scatter.5.cloned.1.call-done = f32[256,1024]{1,0:T(8,128)} async-done(((f32[1024,1024]{1,0:T(8,128)}), f32[256,1024]{1,0:T(8,128)}) %reduce-scatter.5.cloned.1.call-update) | async-done | bytes 1048592 | tf_op jit(solution)/shard_map/reduce_scatter | solution.py:84
  (39 shorter events, 12.5 us)
Async XLA Ops:
  7.2 40.7 %all-gather.5.cloned.1.call-start = ((), (), s32[]{:S(2)}) async-start(), calls=%async_computation.2 | async-start | bytes 2621440 | tf_op jit(solution)/shard_map/all_gather | solution.py:29
  7.9 224.5 %reduce-scatter.3.cloned.1.call-start = ((), (), s32[]{:S(2)}) async-start(), calls=%async_computation.3 | async-start | bytes 18874368 | tf_op jit(solution)/shard_map/reduce_scatter | solution.py:35
  63.9 168.4 %copy-start.1 = (bf16[128,4096]{1,0:T(8,128)(2,1)S(1)}, bf16[128,4096]{1,0:T(8,128)(2,1)}, u32[]{:S(2)}) copy-start(bf16[128,4096]{1,0:T(8,128)(2,1)} %param.9) | copy-start | bytes 3145732
  63.9 168.4 %copy-start.2 = (bf16[128,4096]{1,0:T(8,128)(2,1)S(1)}, bf16[128,4096]{1,0:T(8,128)(2,1)}, u32[]{:S(2)}) copy-start(bf16[128,4096]{1,0:T(8,128)(2,1)} %param.10) | copy-start | bytes 3145732
  64.0 334.7 %all-gather.7.cloned.1.call-start = ((), (), s32[]{:S(2)}) async-start(), calls=%async_computation.4 | async-start | bytes 9437184 | tf_op jit(solution)/shard_map/all_gather | solution.py:43
  236.5 188.0 %all-gather.9.cloned.1.call-start = ((), (), s32[]{:S(2)}) async-start(), calls=%async_computation.6 | async-start | bytes 2621440 | tf_op jit(solution)/shard_map/all_gather | solution.py:28
  237.1 249.4 %all-gather.11.cloned.1.call-start = ((), (), s32[]{:S(2)}) async-start(), calls=%async_computation.7 | async-start | bytes 9437184 | tf_op jit(solution)/shard_map/all_gather | solution.py:42
  237.2 26.8 %collective-permute-start = (bf16[128,4096]{1,0:T(8,128)(2,1)S(1)}, bf16[128,4096]{1,0:T(8,128)(2,1)S(1)}, u32[]{:S(2)}, u32[]{:S(2)}) collective-permute-start(bf16[128,4096]{1,0:T(8,128)(2,1)S(1)} %get-tuple-element.8), channel_id=1, source_target_pairs={{0,4},{4,8},{8,12},{12,16},{16,20},{20,24},{24,28},{28,0},{1,5},{5... | collective-permute-start | bytes 3145736 | tf_op jit(solution)/shard_map/ppermute | solution.py:54
  264.0 49.3 %collective-permute-start.1 = (bf16[128,4096]{1,0:T(8,128)(2,1)S(1)}, bf16[128,4096]{1,0:T(8,128)(2,1)S(1)}, u32[]{:S(2)}, u32[]{:S(2)}) collective-permute-start(bf16[128,4096]{1,0:T(8,128)(2,1)S(1)} %collective-permute-done), channel_id=1, source_target_pairs={{0,4},{4,8},{8,12},{12,16},{16,20},{20,24},{24,28},{28,0},{1,5},{5... | collective-permute-start | bytes 3145736 | tf_op jit(solution)/shard_map/ppermute | solution.py:54
  264.0 276.6 %reduce-scatter.5.cloned.1.call-start = ((), (), s32[]{:S(2)}) async-start(), calls=%async_computation.5 | async-start | bytes 5242880 | tf_op jit(solution)/shard_map/reduce_scatter | solution.py:84
  264.1 49.2 %collective-permute-start.4 = (bf16[128,4096]{1,0:T(8,128)(2,1)S(1)}, bf16[128,4096]{1,0:T(8,128)(2,1)}, u32[]{:S(2)}, u32[]{:S(2)}) collective-permute-start(bf16[128,4096]{1,0:T(8,128)(2,1)S(1)} %get-tuple-element.8), channel_id=1, source_target_pairs={{4,0},{8,4},{12,8},{16,12},{20,16},{24,20},{28,24},{0,28},{5,1},{9... | collective-permute-start | bytes 3145736 | tf_op jit(solution)/shard_map/ppermute | solution.py:57
  313.3 39.7 %collective-permute-start.2 = (bf16[128,4096]{1,0:T(8,128)(2,1)S(1)}, bf16[128,4096]{1,0:T(8,128)(2,1)}, u32[]{:S(2)}, u32[]{:S(2)}) collective-permute-start(bf16[128,4096]{1,0:T(8,128)(2,1)S(1)} %collective-permute-done.1), channel_id=1, source_target_pairs={{0,4},{4,8},{8,12},{12,16},{16,20},{20,24},{24,28},{28,0},{1,5},{5... | collective-permute-start | bytes 3145736 | tf_op jit(solution)/shard_map/ppermute | solution.py:54
  313.3 48.7 %collective-permute-start.5 = (bf16[128,4096]{1,0:T(8,128)(2,1)}, bf16[128,4096]{1,0:T(8,128)(2,1)}, u32[]{:S(2)}, u32[]{:S(2)}) collective-permute-start(bf16[128,4096]{1,0:T(8,128)(2,1)} %collective-permute-done.4), channel_id=1, source_target_pairs={{4,0},{8,4},{12,8},{16,12},{20,16},{24,20},{28,24},{0,28},{5,1},{9... | collective-permute-start | bytes 3145736 | tf_op jit(solution)/shard_map/ppermute | solution.py:57
  352.9 24.2 %collective-permute-start.3 = (bf16[128,4096]{1,0:T(8,128)(2,1)}, bf16[128,4096]{1,0:T(8,128)(2,1)}, u32[]{:S(2)}, u32[]{:S(2)}) collective-permute-start(bf16[128,4096]{1,0:T(8,128)(2,1)} %collective-permute-done.2), channel_id=1, source_target_pairs={{0,4},{4,8},{8,12},{12,16},{16,20},{20,24},{24,28},{28,0},{1,5},{5... | collective-permute-start | bytes 3145736 | tf_op jit(solution)/shard_map/ppermute | solution.py:54
  362.0 27.4 %collective-permute-start.6 = (bf16[128,4096]{1,0:T(8,128)(2,1)}, bf16[128,4096]{1,0:T(8,128)(2,1)S(1)}, u32[]{:S(2)}, u32[]{:S(2)}) collective-permute-start(bf16[128,4096]{1,0:T(8,128)(2,1)} %collective-permute-done.5), channel_id=1, source_target_pairs={{4,0},{8,4},{12,8},{16,12},{20,16},{24,20},{28,24},{0,28},{5,1},{9... | collective-permute-start | bytes 3145736 | tf_op jit(solution)/shard_map/ppermute | solution.py:57
  398.7 12.8 %copy-start = (bf16[8,128,4096]{2,1,0:T(8,128)(2,1)S(1)}, bf16[8,128,4096]{2,1,0:T(8,128)(2,1)}, u32[]{:S(2)}) copy-start(bf16[8,128,4096]{2,1,0:T(8,128)(2,1)} %gather_fusion) | copy-start | bytes 25165828
  439.8 12.1 %copy-start.4 = (bf16[1024,1024]{1,0:T(8,128)(2,1)S(1)}, bf16[1024,1024]{1,0:T(8,128)(2,1)}, u32[]{:S(2)}) copy-start(bf16[1024,1024]{1,0:T(8,128)(2,1)} %all-gather.9.cloned.1.call-done) | copy-start | bytes 6291460
  466.6 19.9 %copy-start.3 = (bf16[1024,1024]{1,0:T(8,128)(2,1)S(1)}, bf16[1024,1024]{1,0:T(8,128)(2,1)}, u32[]{:S(2)}) copy-start(bf16[1024,1024]{1,0:T(8,128)(2,1)} %all-gather.5.cloned.1.call-done) | copy-start | bytes 6291460
Sparse Core Ops, SparseCore 0:
  9.8 38.0 all-gather.4
  64.1 168.2 reduce-scatter.2
  236.7 127.3 all-gather.6
  365.8 37.1 all-gather.8
  404.4 82.0 all-gather.10
  489.3 51.2 reduce-scatter.4
